TPU v7x, 32 devices: a whole 2x2x4 slice. The times are simulated.
32 devices in a mesh: groups: 2 (over x), dp: 16 (over z, y, core).
Axes of the slice: x: 2, y: 2, z: 4, core: 2. Of those that a mesh axis runs over, the one named last changes fastest.
Arguments:
- frames: bfloat16 [128, 256, 1536], P(('groups', 'dp')), parts along dimension 0, may hold values from -6 to 6
- cotangent: bfloat16 [128, 256, 1536], P(('groups', 'dp')), parts along dimension 0, may hold values from -6 to 6
- gain: float32 [1536], replicated, may hold values from 0.25 to 1.75
- down_weight: bfloat16 [320, 1536, 256], P('groups', 'dp'), parts along dimension 0, may hold values from -0.15625 to 0.15625
- up_weight: bfloat16 [320, 1536, 256], P('groups', 'dp'), parts along dimension 0, may hold values from -0.375 to 0.375
- slot_lang: int32 [32, 2], P('groups'), parts along dimension 0, may hold values from 0 to 159
- utt_slot: int32 [128], P('groups'), parts along dimension 0, may hold values from 0 to 1
- lengths: int32 [128], P('groups'), parts along dimension 0, may hold values from 64 to 256
Outputs:
- frame_grads: bfloat16 [128, 256, 1536], P(('groups', 'dp')), parts along dimension 0
- down_grads: bfloat16 [320, 1536, 256], P('groups', 'dp'), parts along dimension 0
- up_grads: bfloat16 [320, 1536, 256], P('groups', 'dp'), parts along dimension 0
There are 2 independent parts, one for each index of `groups`. A program takes and returns all parts, laid end to end along the dimension named above; an argument that names none is the same for every part. Nothing has to cross between parts.
All inputs are finite; a program needn't handle non-finite values.
Results may differ from a plain program's by a relative error of at most 0.0061.
Values may be sent and summed in bfloat16 or wider, within the bound.
No kernel may reach another device: no remote copies, remote signals or barrier semaphores. Data moves between devices by JAX's collectives and lax.ppermute only.
A program may use at most 128 MiB of HBM per device.

v0:
```python
import jax
import jax.numpy as jnp
from jax import lax
from jax.sharding import PartitionSpec as P


def local_pass(frames, cotangent, gain, w_down, w_up, live_mask, slot_select):
    values = frames.astype(jnp.float32)
    centre_mean = jnp.mean(values, axis=2, keepdims=True)
    mean_removed = values - centre_mean
    variance = jnp.mean(mean_removed * mean_removed, axis=2, keepdims=True)
    reciprocal_deviation = lax.rsqrt(variance + 1e-06)
    standardized_input = mean_removed * reciprocal_deviation
    layer_normed = (standardized_input * gain).astype(jnp.bfloat16)
    pre_act = jnp.einsum("ufd,udr->ufr", layer_normed, w_down, preferred_element_type=jnp.float32)
    sigmoid_pre = jax.nn.sigmoid(pre_act)
    hidden = (pre_act * sigmoid_pre).astype(jnp.bfloat16)
    masked_up = jnp.where(live_mask, cotangent, jnp.zeros_like(cotangent))
    hidden_slots = hidden[None] * slot_select[:, :, None, None]
    grad_up = jnp.einsum(
        "ufd,sufr->sdr", masked_up, hidden_slots, preferred_element_type=jnp.float32
    )
    d_hidden = jnp.einsum("ufd,udr->ufr", masked_up, w_up, preferred_element_type=jnp.float32)
    d_pre = (d_hidden * sigmoid_pre * (1.0 + pre_act * (1.0 - sigmoid_pre))).astype(jnp.bfloat16)
    d_pre_slots = d_pre[None] * slot_select[:, :, None, None]
    grad_down = jnp.einsum(
        "ufd,sufr->sdr", layer_normed, d_pre_slots, preferred_element_type=jnp.float32
    )
    d_normed = jnp.einsum("ufr,udr->ufd", d_pre, w_down, preferred_element_type=jnp.float32)
    scaled_rows = d_normed * gain
    inner_gradient = (
        scaled_rows
        - jnp.mean(scaled_rows, axis=2, keepdims=True)
        - standardized_input * jnp.mean(scaled_rows * standardized_input, axis=2, keepdims=True)
    ) * reciprocal_deviation
    d_frames = (cotangent.astype(jnp.float32) + inner_gradient).astype(jnp.bfloat16)
    return (d_frames, grad_down, grad_up)


def on_device(frames, cotangent, gain, down_weight, up_weight, slot_lang, utt_slot, lengths):
    devices = lax.axis_size("dp")
    self_index = lax.axis_index("dp")
    per_device = frames.shape[0]
    slots = slot_lang.shape[1]
    lang_count, row_count, bottleneck = down_weight.shape
    owners = jnp.arange(utt_slot.shape[0], dtype=jnp.int32) // per_device
    utt_lang = slot_lang[owners, utt_slot]
    own_lengths = lax.dynamic_slice_in_dim(lengths, self_index * per_device, per_device)
    own_slot = lax.dynamic_slice_in_dim(utt_slot, self_index * per_device, per_device)
    live_mask = (jnp.arange(frames.shape[1], dtype=jnp.int32)[None, :] < own_lengths[:, None])[
        :, :, None
    ]
    lang_ids = jnp.arange(lang_count, dtype=jnp.int32)
    counts = jnp.sum(jnp.where(utt_lang[None, :] == lang_ids[:, None], lengths[None, :], 0), axis=1)
    scaling = lax.rsqrt(jnp.maximum(counts, 1).astype(jnp.float32))
    member_langs = slot_lang.T.reshape(-1)
    send_down = jnp.take(down_weight, member_langs, axis=0).reshape(
        slots, devices, row_count, bottleneck
    )
    send_up = jnp.take(up_weight, member_langs, axis=0).reshape(
        slots, devices, row_count, bottleneck
    )
    got_down = lax.all_to_all(send_down, "dp", split_axis=1, concat_axis=1, tiled=True)
    got_up = lax.all_to_all(send_up, "dp", split_axis=1, concat_axis=1, tiled=True)
    got_down = got_down.reshape(slots, devices * row_count, bottleneck)
    got_up = got_up.reshape(slots, devices * row_count, bottleneck)
    w_down = jnp.take(got_down, own_slot, axis=0)
    w_up = jnp.take(got_up, own_slot, axis=0)
    slot_select = (jnp.arange(slots, dtype=jnp.int32)[:, None] == own_slot[None, :]).astype(
        jnp.bfloat16
    )
    d_frames, grad_down, grad_up = local_pass(
        frames, cotangent, gain, w_down, w_up, live_mask, slot_select
    )
    own_scale = jnp.take(scaling, lax.dynamic_index_in_dim(slot_lang, self_index, 0, False))
    own_scale = own_scale[:, None, None]

    def exchange_back(grad):
        scaled = (grad * own_scale).astype(jnp.bfloat16)
        scaled = scaled.reshape(slots, devices, row_count, bottleneck)
        back = lax.all_to_all(scaled, "dp", split_axis=1, concat_axis=1, tiled=True)
        return back.reshape(slots * devices, row_count, bottleneck)

    back_down = exchange_back(grad_down)
    back_up = exchange_back(grad_up)
    lang_table = (lang_ids[:, None] == member_langs[None, :]).astype(jnp.bfloat16)
    down_grads = jnp.einsum(
        "lm,mkr->lkr", lang_table, back_down, preferred_element_type=jnp.float32
    ).astype(jnp.bfloat16)
    up_grads = jnp.einsum(
        "lm,mkr->lkr", lang_table, back_up, preferred_element_type=jnp.float32
    ).astype(jnp.bfloat16)
    return (d_frames, down_grads, up_grads)


def solution(mesh):
    placed = (
        P(("groups", "dp"), None, None),
        P(("groups", "dp"), None, None),
        P(),
        P("groups", "dp", None),
        P("groups", "dp", None),
        P("groups", None),
        P("groups"),
        P("groups"),
    )
    return jax.shard_map(
        on_device,
        mesh=mesh,
        in_specs=placed,
        out_specs=(
            P(("groups", "dp"), None, None),
            P("groups", "dp", None),
            P("groups", "dp", None),
        ),
        check_vma=False,
    )
```

profile of v0, /device:TPU:13, one launch (start us, length us, event | category | flops | bytes accessed | tf_op | source)
XLA Modules:
  0.0 215.7 jit_solution(16785040773158458793)
XLA Ops:
  1.4 3.9 %gather_fusion.4 = bf16[32,96,256]{2,1,0:T(8,128)(2,1)S(1)} fusion(bf16[160,96,256]{2,1,0:T(8,128)(2,1)} %param.15, s32[1024]{0:T(1024)S(1)} %pad_clamp_fusion.2), kind=kCustom, calls=%fused_computation.2.clone | custom fusion | bytes 3145856 | tf_op jit(solution)/shard_map/jit(_take)/gather | solution.py:57
  5.3 3.9 %gather_fusion.2 = bf16[32,96,256]{2,1,0:T(8,128)(2,1)S(1)} fusion(bf16[160,96,256]{2,1,0:T(8,128)(2,1)} %param.16, s32[1024]{0:T(1024)S(1)} %pad_clamp_fusion.2), kind=kCustom, calls=%fused_computation.clone | custom fusion | bytes 3145856 | tf_op jit(solution)/shard_map/jit(_take)/gather | solution.py:60
  12.0 6.6 %all-to-all-start.1 = ((bf16[2,16,96,256]{3,2,0,1:T(8,128)(2,1)}), bf16[2,16,96,256]{3,2,0,1:T(8,128)(2,1)}, u32[]{:S(2)}, u32[]{:S(2)}) async-start(bf16[2,16,96,256]{3,2,0,1:T(8,128)(2,1)} %copy.51), calls=%async_computation.1 | async-start | bytes 3145728 | tf_op jit(solution)/shard_map/all_to_all | solution.py:63
  18.6 2.8 %copy.49 = bf16[2,16,96,256]{3,2,0,1:T(8,128)(2,1)} copy(bf16[2,16,96,256]{3,2,1,0:T(8,128)(2,1)} %bitcast.69) | data formatting | bytes 3145728 | tf_op jit(solution)/shard_map/reshape | solution.py:60
  21.4 33.4 %all-to-all-done.1 = bf16[2,16,96,256]{3,2,0,1:T(8,128)(2,1)} async-done(((bf16[2,16,96,256]{3,2,0,1:T(8,128)(2,1)}), bf16[2,16,96,256]{3,2,0,1:T(8,128)(2,1)}, u32[]{:S(2)}, u32[]{:S(2)}) %all-to-all-start.1) | async-done | bytes 1572896 | tf_op jit(solution)/shard_map/all_to_all | solution.py:63
  54.8 4.9 %all-to-all-start = ((bf16[2,16,96,256]{3,2,0,1:T(8,128)(2,1)}), bf16[2,16,96,256]{3,2,0,1:T(8,128)(2,1)}, u32[]{:S(2)}, u32[]{:S(2)}) async-start(bf16[2,16,96,256]{3,2,0,1:T(8,128)(2,1)} %copy.49), calls=%async_computation | async-start | bytes 3145728 | tf_op jit(solution)/shard_map/all_to_all | solution.py:64
  63.3 2.7 %copy.52 = bf16[2,16,96,256]{3,2,1,0:T(8,128)(2,1)} copy(bf16[2,16,96,256]{3,2,0,1:T(8,128)(2,1)} %all-to-all-done.1) | data formatting | bytes 3145728 | tf_op jit(solution)/shard_map/all_to_all | solution.py:63
  66.0 3.8 %gather_fusion.5 = bf16[4,1536,256]{2,1,0:T(8,128)(2,1)} fusion(bf16[2,1536,256]{2,1,0:T(8,128)(2,1)} %bitcast.64, s32[1024]{0:T(1024)S(1)} %pad_clamp_fusion.1), kind=kCustom, calls=%fused_computation.3.clone | custom fusion | bytes 6291472 | tf_op jit(solution)/shard_map/jit(_take)/gather | solution.py:67
  69.8 26.2 %all-to-all-done = bf16[2,16,96,256]{3,2,0,1:T(8,128)(2,1)} async-done(((bf16[2,16,96,256]{3,2,0,1:T(8,128)(2,1)}), bf16[2,16,96,256]{3,2,0,1:T(8,128)(2,1)}, u32[]{:S(2)}, u32[]{:S(2)}) %all-to-all-start) | async-done | bytes 1572896 | tf_op jit(solution)/shard_map/all_to_all | solution.py:64
  96.0 2.7 %copy.50 = bf16[2,16,96,256]{3,2,1,0:T(8,128)(2,1)} copy(bf16[2,16,96,256]{3,2,0,1:T(8,128)(2,1)} %all-to-all-done) | data formatting | bytes 3145728 | tf_op jit(solution)/shard_map/all_to_all | solution.py:64
  98.7 3.8 %gather_fusion.3 = bf16[4,1536,256]{2,1,0:T(8,128)(2,1)} fusion(bf16[2,1536,256]{2,1,0:T(8,128)(2,1)} %bitcast.63, s32[1024]{0:T(1024)S(1)} %pad_clamp_fusion.1), kind=kCustom, calls=%fused_computation.1.clone | custom fusion | bytes 6291472 | tf_op jit(solution)/shard_map/jit(_take)/gather | solution.py:68
  102.5 4.4 %multiply_convert_fusion = (bf16[4,256,256]{2,1,0:T(8,128)(2,1)}, f32[4,256,256]{2,1,0:T(8,128)S(1)}) fusion(bf16[4,1536,256]{2,1,0:T(8,128)(2,1)} %gather_fusion.5, pred[4]{0:T(512)(128)(4,1)S(1)} %get-tuple-element.22, bf16[4,256,1536]{2,1,0:T(8,128)(2,1)S(1)} %copy-done.1, f32[1536]{0:T(1024)S(1)} %copy-done.5, f32[4,256]{1,0:T(4,128)S(1)} %add_rsqrt_fusion, ...), kind=kOutput, calls=%fused_computation.49 | convolution fusion | flops 816054272 | bytes 7878660 | tf_op jit(solution)/shard_map/ufd,udr->ufr/dot_general | solution.py:15
  111.1 4.2 %fusion.28 = bf16[2,1536,256]{1,2,0:T(8,128)(2,1)} fusion(bf16[4,256,1536]{2,1,0:T(8,128)(2,1)S(1)} %copy-done.1, f32[1536]{0:T(1024)S(1)} %copy-done.5, f32[4,256]{1,0:T(4,128)S(1)} %add_rsqrt_fusion, f32[4,256]{1,0:T(4,128)S(1)} %broadcast_multiply_fusion.2, f32[2]{0:T(128)S(1)} %and_select_fusion.1, bf16[2,4]{1,0:T(2,128)(2,1)S(1)} %compare_convert_fusion, ...), kind=kOutput, calls=%fused_computation.37 | convolution fusion | flops 1620574208 | bytes 5257240 | tf_op jit(solution)/shard_map/ufd,sufr->sdr/dot_general | solution.py:26
  117.9 2.7 %copy.55 = bf16[2,16,96,256]{3,2,0,1:T(8,128)(2,1)} copy(bf16[2,16,96,256]{3,2,1,0:T(8,128)(2,1)} %bitcast.66) | data formatting | bytes 3145728 | tf_op jit(solution)/shard_map/reshape | solution.py:80
  120.6 4.9 %all-to-all-start.2 = ((bf16[2,16,96,256]{3,2,0,1:T(8,128)(2,1)}), bf16[2,16,96,256]{3,2,0,1:T(8,128)(2,1)}, u32[]{:S(2)}, u32[]{:S(2)}) async-start(bf16[2,16,96,256]{3,2,0,1:T(8,128)(2,1)} %copy.55), calls=%async_computation.2 | async-start | bytes 3145728 | tf_op jit(solution)/shard_map/all_to_all | solution.py:81
  127.6 5.1 %fusion.25 = bf16[2,1536,256]{1,2,0:T(8,128)(2,1)} fusion(bf16[4,256,1536]{2,1,0:T(8,128)(2,1)} %param.13, pred[4,256]{1,0:T(4,128)(4,1)S(1)} %iota_compare_fusion.2, f32[2]{0:T(128)S(1)} %and_select_fusion.1, bf16[4,256,256]{1,2,0:T(8,128)(2,1)} %copy.57, bf16[2,4]{1,0:T(2,128)(2,1)S(1)} %compare_convert_fusion), kind=kOutput, calls=%fused_computation.36 | convolution fusion | flops 1614282752 | bytes 5243928 | tf_op jit(solution)/shard_map/ufd,sufr->sdr/dot_general | solution.py:20
  135.2 2.7 %copy.59 = bf16[2,16,96,256]{3,2,0,1:T(8,128)(2,1)} copy(bf16[2,16,96,256]{3,2,1,0:T(8,128)(2,1)} %bitcast.67) | data formatting | bytes 3145728 | tf_op jit(solution)/shard_map/reshape | solution.py:80
  137.9 23.9 %all-to-all-done.2 = bf16[2,16,96,256]{3,2,0,1:T(8,128)(2,1)} async-done(((bf16[2,16,96,256]{3,2,0,1:T(8,128)(2,1)}), bf16[2,16,96,256]{3,2,0,1:T(8,128)(2,1)}, u32[]{:S(2)}, u32[]{:S(2)}) %all-to-all-start.2) | async-done | bytes 1572896 | tf_op jit(solution)/shard_map/all_to_all | solution.py:81
  161.8 4.9 %all-to-all-start.3 = ((bf16[2,16,96,256]{3,2,0,1:T(8,128)(2,1)}), bf16[2,16,96,256]{3,2,0,1:T(8,128)(2,1)}, u32[]{:S(2)}, u32[]{:S(2)}) async-start(bf16[2,16,96,256]{3,2,0,1:T(8,128)(2,1)} %copy.59), calls=%async_computation.3 | async-start | bytes 3145728 | tf_op jit(solution)/shard_map/all_to_all | solution.py:81
  166.7 4.6 %multiply_reduce_fusion = (f32[4,256]{1,0:T(4,128)S(1)}, f32[4,256]{1,0:T(4,128)S(1)}, f32[4,256,1536]{2,1,0:T(8,128)S(1)}) fusion(f32[1536]{0:T(1024)S(1)} %copy-done.5, f32[4,256]{1,0:T(4,128)S(1)} %add_rsqrt_fusion, f32[4,256]{1,0:T(4,128)S(1)} %broadcast_multiply_fusion.2, bf16[4,256,1536]{2,1,0:T(8,128)(2,1)S(1)} %copy-done.1, ...), kind=kOutput, calls=%fused_computation.22 | convolution fusion | flops 817887232 | bytes 13129732 | tf_op jit(solution)/shard_map/ufr,udr->ufd/dot_general | solution.py:29
  171.4 4.0 %fusion.10 = bf16[4,256,1536]{2,1,0:T(8,128)(2,1)} fusion(bf16[4,256,1536]{2,1,0:T(8,128)(2,1)S(1)} %copy-done.1, bf16[4,256,1536]{2,1,0:T(8,128)(2,1)S(1)} %copy-done.4, f32[4,256,1536]{2,1,0:T(8,128)S(1)} %get-tuple-element.26, f32[4,256]{1,0:T(4,128)S(1)} %get-tuple-element.29, f32[4,256]{1,0:T(4,128)S(1)} %get-tuple-element.30, f32[1536]{0:T(1024)S(1)} %copy-done.5, ...), kind=kLoop, calls=%fused_computation.20 | loop fusion | flops 17301504 | bytes 15751168 | tf_op jit(solution)/shard_map/convert_element_type | solution.py:36
  179.9 7.8 %copy.61 = bf16[160,96,256]{2,1,0:T(8,128)(2,1)} copy(bf16[160,96,256]{2,0,1:T(8,128)(2,1)S(1)} %convolution_convert_fusion.1) | data formatting | bytes 15728640
  187.7 15.3 %all-to-all-done.3 = bf16[2,16,96,256]{3,2,0,1:T(8,128)(2,1)} async-done(((bf16[2,16,96,256]{3,2,0,1:T(8,128)(2,1)}), bf16[2,16,96,256]{3,2,0,1:T(8,128)(2,1)}, u32[]{:S(2)}, u32[]{:S(2)}) %all-to-all-start.3) | async-done | bytes 1572896 | tf_op jit(solution)/shard_map/all_to_all | solution.py:81
  207.6 8.1 %copy.62 = bf16[160,96,256]{2,1,0:T(8,128)(2,1)} copy(bf16[160,96,256]{2,0,1:T(8,128)(2,1)S(1)} %convolution_convert_fusion) | data formatting | bytes 15728640
  (51 shorter events, 27.7 us)
Async XLA Ops:
  12.0 42.8 %all-to-all-start.1 = ((bf16[2,16,96,256]{3,2,0,1:T(8,128)(2,1)}), bf16[2,16,96,256]{3,2,0,1:T(8,128)(2,1)}, u32[]{:S(2)}, u32[]{:S(2)}) async-start(bf16[2,16,96,256]{3,2,0,1:T(8,128)(2,1)} %copy.51), calls=%async_computation.1 | async-start | bytes 3145728 | tf_op jit(solution)/shard_map/all_to_all | solution.py:63
  18.5 41.2 %copy-start.7 = (s32[64]{0:T(128)S(1)}, s32[64]{0:T(128)}, u32[]{:S(2)}) copy-start(s32[64]{0:T(128)} %param.18) | copy-start | bytes 772
  18.5 41.2 %copy-start = (s32[16,2]{0,1:T(2,128)S(1)}, s32[16,2]{0,1:T(2,128)}, u32[]{:S(2)}) copy-start(s32[16,2]{0,1:T(2,128)} %param.17) | copy-start | bytes 388
  18.5 42.3 %copy-start.6 = (s32[64]{0:T(128)S(1)}, s32[64]{0:T(128)}, u32[]{:S(2)}) copy-start(s32[64]{0:T(128)} %param.19) | copy-start | bytes 772
  18.5 43.3 %copy-start.1 = (bf16[4,256,1536]{2,1,0:T(8,128)(2,1)S(1)}, bf16[4,256,1536]{2,1,0:T(8,128)(2,1)}, u32[]{:S(2)}) copy-start(bf16[4,256,1536]{2,1,0:T(8,128)(2,1)} %param.12) | copy-start | bytes 9437188
  54.8 41.2 %all-to-all-start = ((bf16[2,16,96,256]{3,2,0,1:T(8,128)(2,1)}), bf16[2,16,96,256]{3,2,0,1:T(8,128)(2,1)}, u32[]{:S(2)}, u32[]{:S(2)}) async-start(bf16[2,16,96,256]{3,2,0,1:T(8,128)(2,1)} %copy.49), calls=%async_computation | async-start | bytes 3145728 | tf_op jit(solution)/shard_map/all_to_all | solution.py:64
  98.7 3.8 %copy-start.5 = (f32[1536]{0:T(1024)S(1)}, f32[1536]{0:T(1024)}, u32[]{:S(2)}) copy-start(f32[1536]{0:T(1024)} %param.14) | copy-start | bytes 18436
  102.5 4.4 %copy-start.2 = (bf16[4,1536,256]{2,1,0:T(8,128)(2,1)S(1)}, bf16[4,1536,256]{2,1,0:T(8,128)(2,1)}, u32[]{:S(2)}) copy-start(bf16[4,1536,256]{2,1,0:T(8,128)(2,1)} %gather_fusion.3) | copy-start | bytes 9437188
  102.5 4.4 %copy-start.3 = (bf16[4,256,1536]{2,1,0:T(8,128)(2,1)S(1)}, bf16[4,256,1536]{2,1,0:T(8,128)(2,1)}, u32[]{:S(2)}) copy-start(bf16[4,256,1536]{2,1,0:T(8,128)(2,1)} %param.13) | copy-start | bytes 9437188
  120.6 41.2 %all-to-all-start.2 = ((bf16[2,16,96,256]{3,2,0,1:T(8,128)(2,1)}), bf16[2,16,96,256]{3,2,0,1:T(8,128)(2,1)}, u32[]{:S(2)}, u32[]{:S(2)}) async-start(bf16[2,16,96,256]{3,2,0,1:T(8,128)(2,1)} %copy.55), calls=%async_computation.2 | async-start | bytes 3145728 | tf_op jit(solution)/shard_map/all_to_all | solution.py:81
  161.8 41.2 %all-to-all-start.3 = ((bf16[2,16,96,256]{3,2,0,1:T(8,128)(2,1)}), bf16[2,16,96,256]{3,2,0,1:T(8,128)(2,1)}, u32[]{:S(2)}, u32[]{:S(2)}) async-start(bf16[2,16,96,256]{3,2,0,1:T(8,128)(2,1)} %copy.59), calls=%async_computation.3 | async-start | bytes 3145728 | tf_op jit(solution)/shard_map/all_to_all | solution.py:81
  166.7 4.6 %copy-start.4 = (bf16[4,256,1536]{2,1,0:T(8,128)(2,1)S(1)}, bf16[4,256,1536]{2,1,0:T(8,128)(2,1)}, u32[]{:S(2)}) copy-start(bf16[4,256,1536]{2,1,0:T(8,128)(2,1)} %param.13) | copy-start | bytes 9437188
where the time goes:
time: 217 us; the launch traced here: 216 us
  waiting for transfers between devices  98.8 us (46%)
  local copies, waits for them, and re-layouts  62.5 us (29%)
  matrix products  25.1 us (12%)
  starting transfers between devices  21.3 us (10%)
  other arithmetic  7.25 us (3%)
    all_to_all x2, waiting for transfers between devices, exchange_back(): back = lax.all_to_all(scaled, 'dp', split_axis=1, concat_axis=1, tiled=True)  39.2 us
    all_to_all x1, waiting for transfers between devices, on_device(): lax.all_to_all(send_down, 'dp', split_axis=1, concat_axis=1, tiled=True)  33.4 us
    all_to_all x1, waiting for transfers between devices, on_device(): lax.all_to_all(send_up, 'dp', split_axis=1, concat_axis=1, tiled=True)  26.2 us
    unnamed x18, local copies, waits for them, and re-layouts  15.9 us
    all_to_all x2, starting transfers between devices, exchange_back(): back = lax.all_to_all(scaled, 'dp', split_axis=1, concat_axis=1, tiled=True)  9.83 us
    all_to_all x1, starting transfers between devices, on_device(): lax.all_to_all(send_down, 'dp', split_axis=1, concat_axis=1, tiled=True)  6.55 us
    reshape x2, local copies, waits for them, and re-layouts, exchange_back(): scaled = scaled.reshape(slots, devices, row_count, bottleneck)  5.37 us
    convert_element_type x2, local copies, waits for them, and re-layouts, exchange_back(): scaled = (grad * own_scale).astype(jnp.bfloat16)  5.15 us
  transfers between devices with their start and end apart: 4, of which 4 were waited for; matrix products, arithmetic and copies ran while one was open for 21% of the time, Pallas kernels for 0%

commit v1 on v0

--- a/solution.py
+++ b/solution.py
@@ -2,6 +2,14 @@
 import jax.numpy as jnp
 from jax import lax
 from jax.sharding import PartitionSpec as P
+
+
+def watch_the_panel(w_in, row_axis):
+    reached = lax.axis_size(row_axis)
+    m_next = jnp.split(w_in, reached, 1)
+    item_now = jnp.stack(m_next)
+    z2 = lax.all_to_all(item_now, axis_name=row_axis, split_axis=0, concat_axis=0)
+    return jnp.concatenate(z2, 1)
 
 
 def local_pass(frames, cotangent, gain, w_down, w_up, live_mask, slot_select):
@@ -61,7 +69,7 @@
         slots, devices, row_count, bottleneck
     )
     got_down = lax.all_to_all(send_down, "dp", split_axis=1, concat_axis=1, tiled=True)
-    got_up = lax.all_to_all(send_up, "dp", split_axis=1, concat_axis=1, tiled=True)
+    got_up = watch_the_panel(send_up, "dp")
     got_down = got_down.reshape(slots, devices * row_count, bottleneck)
     got_up = got_up.reshape(slots, devices * row_count, bottleneck)
     w_down = jnp.take(got_down, own_slot, axis=0)

time: 217 us -> 229 us (1.055)
  local copies, waits for them, and re-layouts: 62.5 us -> 71.6 us
  waiting for transfers between devices: 98.8 us -> 103 us
    unnamed x18 -> x33, local copies, waits for them, and re-layouts: 15.9 us -> 25.6 us
    all_to_all x1, waiting for transfers between devices: 26.2 us -> 33.2 us  [watch_the_panel(): lax.all_to_all(item_now, axis_name=row_axis, split_axis=0, concat_axis=0)]
    all_to_all x1, waiting for transfers between devices: 33.4 us -> 30.2 us  [on_device(): lax.all_to_all(send_down, 'dp', split_axis=1, concat_axis=1, tiled=True)]
    all_to_all x1 -> x0, local copies, waits for them, and re-layouts: 2.66 us -> none  [on_device(): lax.all_to_all(send_up, 'dp', split_axis=1, concat_axis=1, tiled=True)]
  transfers between devices with their start and end apart: 4 -> 4, of which waited for: 4 -> 4; matrix products, arithmetic and copies ran while one was open for 21% -> 19% of each run, Pallas kernels for 0% -> 0%
where the time goes in v1:
time: 229 us; the launch traced here: 228 us
  waiting for transfers between devices  103 us (45%)
  local copies, waits for them, and re-layouts  71.6 us (31%)
  matrix products  24.9 us (11%)
  starting transfers between devices  21.3 us (9%)
  other arithmetic  7.19 us (3%)
    all_to_all x2, waiting for transfers between devices, exchange_back(): back = lax.all_to_all(scaled, 'dp', split_axis=1, concat_axis=1, tiled=True)  39.2 us
    all_to_all x1, waiting for transfers between devices, watch_the_panel(): lax.all_to_all(item_now, axis_name=row_axis, split_axis=0, concat_axis=0)  33.2 us
    all_to_all x1, waiting for transfers between devices, on_device(): lax.all_to_all(send_down, 'dp', split_axis=1, concat_axis=1, tiled=True)  30.2 us
    unnamed x33, local copies, waits for them, and re-layouts  25.6 us
    all_to_all x2, starting transfers between devices, exchange_back(): back = lax.all_to_all(scaled, 'dp', split_axis=1, concat_axis=1, tiled=True)  9.81 us
    all_to_all x1, starting transfers between devices, watch_the_panel(): lax.all_to_all(item_now, axis_name=row_axis, split_axis=0, concat_axis=0)  6.55 us
    reshape x2, local copies, waits for them, and re-layouts, exchange_back(): scaled = scaled.reshape(slots, devices, row_count, bottleneck)  5.37 us
    convert_element_type x2, local copies, waits for them, and re-layouts, exchange_back(): scaled = (grad * own_scale).astype(jnp.bfloat16)  5.15 us
  transfers between devices with their start and end apart: 4, of which 4 were waited for; matrix products, arithmetic and copies ran while one was open for 19% of the time, Pallas kernels for 0%

profile of v1, /device:TPU:13, one launch (start us, length us, event | category | flops | bytes accessed | tf_op | source)
XLA Modules:
  0.0 228.4 jit_solution(17932134935132733881)
XLA Ops:
  1.4 3.9 %gather_fusion.4 = bf16[32,96,256]{2,1,0:T(8,128)(2,1)S(1)} fusion(bf16[160,96,256]{2,1,0:T(8,128)(2,1)} %param.15, s32[1024]{0:T(1024)S(1)} %pad_clamp_fusion.2), kind=kCustom, calls=%fused_computation.2.clone | custom fusion | bytes 3145856 | tf_op jit(solution)/shard_map/jit(_take)/gather | solution.py:65
  5.3 3.9 %gather_fusion.2 = bf16[32,96,256]{2,1,0:T(8,128)(2,1)S(1)} fusion(bf16[160,96,256]{2,1,0:T(8,128)(2,1)} %param.16, s32[1024]{0:T(1024)S(1)} %pad_clamp_fusion.2), kind=kCustom, calls=%fused_computation.clone | custom fusion | bytes 3145856 | tf_op jit(solution)/shard_map/jit(_take)/gather | solution.py:68
  21.0 6.6 %all-to-all-start = ((bf16[16,2,1,96,256]{4,3,1,2,0:T(8,128)(2,1)}), bf16[16,2,1,96,256]{4,3,1,2,0:T(8,128)(2,1)}, u32[]{:S(2)}, u32[]{:S(2)}) async-start(bf16[16,2,1,96,256]{4,3,1,2,0:T(8,128)(2,1)} %fusion.53), calls=%async_computation | async-start | bytes 3145728 | tf_op jit(solution)/shard_map/all_to_all | solution.py:11
  27.8 2.8 %copy.149 = bf16[2,16,96,256]{3,2,0,1:T(8,128)(2,1)} copy(bf16[2,16,96,256]{3,2,1,0:T(8,128)(2,1)} %bitcast.164) | data formatting | bytes 3145728 | tf_op jit(solution)/shard_map/reshape | solution.py:65
  30.7 33.2 %all-to-all-done = bf16[16,2,1,96,256]{4,3,1,2,0:T(8,128)(2,1)} async-done(((bf16[16,2,1,96,256]{4,3,1,2,0:T(8,128)(2,1)}), bf16[16,2,1,96,256]{4,3,1,2,0:T(8,128)(2,1)}, u32[]{:S(2)}, u32[]{:S(2)}) %all-to-all-start) | async-done | bytes 1572896 | tf_op jit(solution)/shard_map/all_to_all | solution.py:11
  63.9 4.9 %all-to-all-start.1 = ((bf16[2,16,96,256]{3,2,0,1:T(8,128)(2,1)}), bf16[2,16,96,256]{3,2,0,1:T(8,128)(2,1)}, u32[]{:S(2)}, u32[]{:S(2)}) async-start(bf16[2,16,96,256]{3,2,0,1:T(8,128)(2,1)} %copy.149), calls=%async_computation.1 | async-start | bytes 3145728 | tf_op jit(solution)/shard_map/all_to_all | solution.py:71
  72.2 2.7 %copy.148 = bf16[2,16,1,96,256]{4,3,1,0,2:T(8,128)(2,1)} copy(bf16[2,16,1,96,256]{4,3,0,2,1:T(8,128)(2,1)} %bitcast.18) | data formatting | bytes 3145728 | tf_op jit(solution)/shard_map/reshape | solution.py:12
  74.9 30.2 %all-to-all-done.1 = bf16[2,16,96,256]{3,2,0,1:T(8,128)(2,1)} async-done(((bf16[2,16,96,256]{3,2,0,1:T(8,128)(2,1)}), bf16[2,16,96,256]{3,2,0,1:T(8,128)(2,1)}, u32[]{:S(2)}, u32[]{:S(2)}) %all-to-all-start.1) | async-done | bytes 1572896 | tf_op jit(solution)/shard_map/all_to_all | solution.py:71
  105.1 2.7 %copy.150 = bf16[2,16,96,256]{3,2,1,0:T(8,128)(2,1)} copy(bf16[2,16,96,256]{3,2,0,1:T(8,128)(2,1)} %all-to-all-done.1) | data formatting | bytes 3145728 | tf_op jit(solution)/shard_map/all_to_all | solution.py:71
  107.8 3.8 %gather_fusion.5 = bf16[4,1536,256]{2,1,0:T(8,128)(2,1)} fusion(bf16[2,1536,256]{2,1,0:T(8,128)(2,1)} %bitcast.159, s32[1024]{0:T(1024)S(1)} %get-tuple-element.33), kind=kCustom, calls=%fused_computation.3.clone | custom fusion | bytes 6291472 | tf_op jit(solution)/shard_map/jit(_take)/gather | solution.py:75
  111.6 3.8 %gather_fusion.3 = bf16[4,1536,256]{2,1,0:T(8,128)(2,1)} fusion(bf16[2,1536,256]{2,1,0:T(8,128)(2,1)} %bitcast.158, s32[1024]{0:T(1024)S(1)} %get-tuple-element.33), kind=kCustom, calls=%fused_computation.1.clone | custom fusion | bytes 6291472 | tf_op jit(solution)/shard_map/jit(_take)/gather | solution.py:76
  115.4 4.4 %multiply_convert_fusion = (bf16[4,256,256]{2,1,0:T(8,128)(2,1)}, f32[4,256,256]{2,1,0:T(8,128)S(1)}) fusion(bf16[4,1536,256]{2,1,0:T(8,128)(2,1)} %gather_fusion.5, pred[4]{0:T(512)(128)(4,1)S(1)} %get-tuple-element.25, bf16[4,256,1536]{2,1,0:T(8,128)(2,1)S(1)} %copy-done.1, f32[1536]{0:T(1024)S(1)} %copy-done.5, f32[4,256]{1,0:T(4,128)S(1)} %add_rsqrt_fusion, ...), kind=kOutput, calls=%fused_computation.49 | convolution fusion | flops 816054272 | bytes 7878660 | tf_op jit(solution)/shard_map/ufd,udr->ufr/dot_general | solution.py:23
  124.0 4.1 %fusion.28 = bf16[2,1536,256]{1,2,0:T(8,128)(2,1)} fusion(bf16[4,256,1536]{2,1,0:T(8,128)(2,1)S(1)} %copy-done.1, f32[1536]{0:T(1024)S(1)} %copy-done.5, f32[4,256]{1,0:T(4,128)S(1)} %add_rsqrt_fusion, f32[4,256]{1,0:T(4,128)S(1)} %broadcast_multiply_fusion.2, f32[2]{0:T(128)S(1)} %and_select_fusion.1, bf16[2,4]{1,0:T(2,128)(2,1)S(1)} %compare_convert_fusion, ...), kind=kOutput, calls=%fused_computation.37 | convolution fusion | flops 1620574208 | bytes 5257240 | tf_op jit(solution)/shard_map/ufd,sufr->sdr/dot_general | solution.py:34
  130.7 2.7 %copy.153 = bf16[2,16,96,256]{3,2,0,1:T(8,128)(2,1)} copy(bf16[2,16,96,256]{3,2,1,0:T(8,128)(2,1)} %bitcast.161) | data formatting | bytes 3145728 | tf_op jit(solution)/shard_map/reshape | solution.py:88
  133.4 4.9 %all-to-all-start.2 = ((bf16[2,16,96,256]{3,2,0,1:T(8,128)(2,1)}), bf16[2,16,96,256]{3,2,0,1:T(8,128)(2,1)}, u32[]{:S(2)}, u32[]{:S(2)}) async-start(bf16[2,16,96,256]{3,2,0,1:T(8,128)(2,1)} %copy.153), calls=%async_computation.2 | async-start | bytes 3145728 | tf_op jit(solution)/shard_map/all_to_all | solution.py:89
  140.3 5.1 %fusion.25 = bf16[2,1536,256]{1,2,0:T(8,128)(2,1)} fusion(bf16[4,256,1536]{2,1,0:T(8,128)(2,1)} %param.13, pred[4,256]{1,0:T(4,128)(4,1)S(1)} %iota_compare_fusion.2, f32[2]{0:T(128)S(1)} %and_select_fusion.1, bf16[4,256,256]{1,2,0:T(8,128)(2,1)} %copy.155, bf16[2,4]{1,0:T(2,128)(2,1)S(1)} %compare_convert_fusion), kind=kOutput, calls=%fused_computation.36 | convolution fusion | flops 1614282752 | bytes 5243928 | tf_op jit(solution)/shard_map/ufd,sufr->sdr/dot_general | solution.py:28
  148.0 2.7 %copy.157 = bf16[2,16,96,256]{3,2,0,1:T(8,128)(2,1)} copy(bf16[2,16,96,256]{3,2,1,0:T(8,128)(2,1)} %bitcast.162) | data formatting | bytes 3145728 | tf_op jit(solution)/shard_map/reshape | solution.py:88
  150.7 23.9 %all-to-all-done.2 = bf16[2,16,96,256]{3,2,0,1:T(8,128)(2,1)} async-done(((bf16[2,16,96,256]{3,2,0,1:T(8,128)(2,1)}), bf16[2,16,96,256]{3,2,0,1:T(8,128)(2,1)}, u32[]{:S(2)}, u32[]{:S(2)}) %all-to-all-start.2) | async-done | bytes 1572896 | tf_op jit(solution)/shard_map/all_to_all | solution.py:89
  174.6 4.9 %all-to-all-start.3 = ((bf16[2,16,96,256]{3,2,0,1:T(8,128)(2,1)}), bf16[2,16,96,256]{3,2,0,1:T(8,128)(2,1)}, u32[]{:S(2)}, u32[]{:S(2)}) async-start(bf16[2,16,96,256]{3,2,0,1:T(8,128)(2,1)} %copy.157), calls=%async_computation.3 | async-start | bytes 3145728 | tf_op jit(solution)/shard_map/all_to_all | solution.py:89
  179.5 4.6 %multiply_reduce_fusion = (f32[4,256]{1,0:T(4,128)S(1)}, f32[4,256]{1,0:T(4,128)S(1)}, f32[4,256,1536]{2,1,0:T(8,128)S(1)}) fusion(f32[1536]{0:T(1024)S(1)} %copy-done.5, f32[4,256]{1,0:T(4,128)S(1)} %add_rsqrt_fusion, f32[4,256]{1,0:T(4,128)S(1)} %broadcast_multiply_fusion.2, bf16[4,256,1536]{2,1,0:T(8,128)(2,1)S(1)} %copy-done.1, ...), kind=kOutput, calls=%fused_computation.22 | convolution fusion | flops 817887232 | bytes 13129732 | tf_op jit(solution)/shard_map/ufr,udr->ufd/dot_general | solution.py:37
  184.1 3.9 %fusion.10 = bf16[4,256,1536]{2,1,0:T(8,128)(2,1)} fusion(bf16[4,256,1536]{2,1,0:T(8,128)(2,1)S(1)} %copy-done.1, bf16[4,256,1536]{2,1,0:T(8,128)(2,1)S(1)} %copy-done.4, f32[4,256,1536]{2,1,0:T(8,128)S(1)} %get-tuple-element.29, f32[4,256]{1,0:T(4,128)S(1)} %broadcast_multiply_fusion, f32[4,256]{1,0:T(4,128)S(1)} %broadcast_multiply_fusion.1, ...), kind=kLoop, calls=%fused_computation.20 | loop fusion | flops 17301504 | bytes 15751168 | tf_op jit(solution)/shard_map/convert_element_type | solution.py:44
  192.6 7.8 %copy.159 = bf16[160,96,256]{2,1,0:T(8,128)(2,1)} copy(bf16[160,96,256]{2,0,1:T(8,128)(2,1)S(1)} %convolution_convert_fusion.1) | data formatting | bytes 15728640
  200.4 15.4 %all-to-all-done.3 = bf16[2,16,96,256]{3,2,0,1:T(8,128)(2,1)} async-done(((bf16[2,16,96,256]{3,2,0,1:T(8,128)(2,1)}), bf16[2,16,96,256]{3,2,0,1:T(8,128)(2,1)}, u32[]{:S(2)}, u32[]{:S(2)}) %all-to-all-start.3) | async-done | bytes 1572896 | tf_op jit(solution)/shard_map/all_to_all | solution.py:89
  220.4 8.1 %copy.160 = bf16[160,96,256]{2,1,0:T(8,128)(2,1)} copy(bf16[160,96,256]{2,0,1:T(8,128)(2,1)S(1)} %convolution_convert_fusion) | data formatting | bytes 15728640
  (66 shorter events, 36.8 us)
Async XLA Ops:
  10.7 16.9 %copy-start = (s32[16,2]{0,1:T(2,128)S(1)}, s32[16,2]{0,1:T(2,128)}, u32[]{:S(2)}) copy-start(s32[16,2]{0,1:T(2,128)} %param.17) | copy-start | bytes 388
  21.0 42.8 %all-to-all-start = ((bf16[16,2,1,96,256]{4,3,1,2,0:T(8,128)(2,1)}), bf16[16,2,1,96,256]{4,3,1,2,0:T(8,128)(2,1)}, u32[]{:S(2)}, u32[]{:S(2)}) async-start(bf16[16,2,1,96,256]{4,3,1,2,0:T(8,128)(2,1)} %fusion.53), calls=%async_computation | async-start | bytes 3145728 | tf_op jit(solution)/shard_map/all_to_all | solution.py:11
  27.8 41.0 %copy-start.6 = (s32[64]{0:T(128)S(1)}, s32[64]{0:T(128)}, u32[]{:S(2)}) copy-start(s32[64]{0:T(128)} %param.18) | copy-start | bytes 772
  27.8 41.9 %copy-start.7 = (s32[64]{0:T(128)S(1)}, s32[64]{0:T(128)}, u32[]{:S(2)}) copy-start(s32[64]{0:T(128)} %param.19) | copy-start | bytes 772
  27.8 42.9 %copy-start.1 = (bf16[4,256,1536]{2,1,0:T(8,128)(2,1)S(1)}, bf16[4,256,1536]{2,1,0:T(8,128)(2,1)}, u32[]{:S(2)}) copy-start(bf16[4,256,1536]{2,1,0:T(8,128)(2,1)} %param.12) | copy-start | bytes 9437188
  63.9 41.2 %all-to-all-start.1 = ((bf16[2,16,96,256]{3,2,0,1:T(8,128)(2,1)}), bf16[2,16,96,256]{3,2,0,1:T(8,128)(2,1)}, u32[]{:S(2)}, u32[]{:S(2)}) async-start(bf16[2,16,96,256]{3,2,0,1:T(8,128)(2,1)} %copy.149), calls=%async_computation.1 | async-start | bytes 3145728 | tf_op jit(solution)/shard_map/all_to_all | solution.py:71
  111.6 3.8 %copy-start.5 = (f32[1536]{0:T(1024)S(1)}, f32[1536]{0:T(1024)}, u32[]{:S(2)}) copy-start(f32[1536]{0:T(1024)} %param.14) | copy-start | bytes 18436
  115.4 4.4 %copy-start.2 = (bf16[4,1536,256]{2,1,0:T(8,128)(2,1)S(1)}, bf16[4,1536,256]{2,1,0:T(8,128)(2,1)}, u32[]{:S(2)}) copy-start(bf16[4,1536,256]{2,1,0:T(8,128)(2,1)} %gather_fusion.3) | copy-start | bytes 9437188
  115.4 4.4 %copy-start.3 = (bf16[4,256,1536]{2,1,0:T(8,128)(2,1)S(1)}, bf16[4,256,1536]{2,1,0:T(8,128)(2,1)}, u32[]{:S(2)}) copy-start(bf16[4,256,1536]{2,1,0:T(8,128)(2,1)} %param.13) | copy-start | bytes 9437188
  133.4 41.2 %all-to-all-start.2 = ((bf16[2,16,96,256]{3,2,0,1:T(8,128)(2,1)}), bf16[2,16,96,256]{3,2,0,1:T(8,128)(2,1)}, u32[]{:S(2)}, u32[]{:S(2)}) async-start(bf16[2,16,96,256]{3,2,0,1:T(8,128)(2,1)} %copy.153), calls=%async_computation.2 | async-start | bytes 3145728 | tf_op jit(solution)/shard_map/all_to_all | solution.py:89
  174.6 41.2 %all-to-all-start.3 = ((bf16[2,16,96,256]{3,2,0,1:T(8,128)(2,1)}), bf16[2,16,96,256]{3,2,0,1:T(8,128)(2,1)}, u32[]{:S(2)}, u32[]{:S(2)}) async-start(bf16[2,16,96,256]{3,2,0,1:T(8,128)(2,1)} %copy.157), calls=%async_computation.3 | async-start | bytes 3145728 | tf_op jit(solution)/shard_map/all_to_all | solution.py:89
  179.5 4.6 %copy-start.4 = (bf16[4,256,1536]{2,1,0:T(8,128)(2,1)S(1)}, bf16[4,256,1536]{2,1,0:T(8,128)(2,1)}, u32[]{:S(2)}) copy-start(bf16[4,256,1536]{2,1,0:T(8,128)(2,1)} %param.13) | copy-start | bytes 9437188
